TPU v7x, 512 devices: a whole 4x4x16 slice. The times are simulated.
512 devices in a mesh: expert: 32 (over x, y, core), replica: 16 (over z).
Axes of the slice: x: 4, y: 4, z: 16, core: 2. Of those that a mesh axis runs over, the one named last changes fastest.
Arguments:
- tokens: bfloat16 [65536, 2560], P(('expert', 'replica')), may hold values from -6 to 6
- cotangent: bfloat16 [65536, 2560], P(('expert', 'replica')), may hold values from -4 to 4
- partner: int32 [65536, 1], P(('expert', 'replica')), may hold values from 0 to 31; in each aligned block of 128 rows (0 to 127, 128 to 255, ...) at most 5 rows name the same one
- combine: int32 [65536, 2], P(('expert', 'replica')), may hold values from 1 to 8
- counts: int32 [512], P(('expert', 'replica')), may hold values from 32 to 128, as said below
- w_gate: bfloat16 [32, 2560, 768], P('expert', 'replica'), may hold values from -0.125 to 0.125
- w_up: bfloat16 [32, 2560, 768], P('expert', 'replica'), may hold values from -0.125 to 0.125
- w_down: bfloat16 [32, 768, 2560], P('expert', 'replica'), may hold values from -0.21875 to 0.21875
Outputs:
- token_grad: bfloat16 [65536, 2560], P(('expert', 'replica'))
- grad_down: bfloat16 [32, 768, 2560], P('expert', 'replica')
Inputs may be any that keep to these rules, and one draw needn't show every extreme that they name: `partner`: within the 128 rows of one device no expert index is named by more than 5 rows, and some device names one exactly 5 times. `counts`: some device has all 128 slots real.
All inputs are finite; a program needn't handle non-finite values.
Results may differ from a plain program's by a relative error of at most 0.017.
Values may be sent and summed in bfloat16 or wider, within the bound.
No kernel may reach another device: no remote copies, remote signals or barrier semaphores. Data moves between devices by JAX's collectives and lax.ppermute only.
A program may use at most 64 MiB of HBM per device.

v0:
```python
import jax
import jax.numpy as jnp
from jax import lax
from jax.sharding import PartitionSpec as P


def against_rows(left, matrix):
    return lax.dot_general(
        left, matrix, (((1,), (1,)), ((), ())), preferred_element_type=jnp.float32
    )


def expert_backward(inputs, upstream, gate_w, up_w, down_w):
    gate_act = jnp.dot(inputs, gate_w, preferred_element_type=jnp.float32)
    up_act = jnp.dot(inputs, up_w, preferred_element_type=jnp.float32)
    sigmoid_gate = jax.nn.sigmoid(gate_act)
    swish_gate = gate_act * sigmoid_gate
    hidden = (swish_gate * up_act).astype(jnp.bfloat16)
    hidden_grad = against_rows(upstream, down_w)
    gate_grad = (
        hidden_grad * up_act * sigmoid_gate * (1.0 + gate_act * (1.0 - sigmoid_gate))
    ).astype(jnp.bfloat16)
    up_grad = (hidden_grad * swish_gate).astype(jnp.bfloat16)
    input_grad = against_rows(gate_grad, gate_w) + against_rows(up_grad, up_w)
    return (hidden, input_grad)


def local(tokens, cotangent, partner, combine, counts, w_gate, w_up, w_down):
    tok_rows = tokens.shape[0]
    width = tokens.shape[1]
    expert_count = lax.axis_size("expert")
    capacity = max(2, (5 * tok_rows // 4 + expert_count - 1) // expert_count)
    positions = jnp.arange(tok_rows, dtype=jnp.int32)
    valid_rows = positions < counts[0]
    weights = combine.astype(jnp.float32)
    weight_sum = weights[:, 0] + weights[:, 1]
    share_home = jnp.where(valid_rows, weights[:, 0] / weight_sum, 0.0)
    share_away = jnp.where(valid_rows, weights[:, 1] / weight_sum, 0.0)
    upstream = cotangent.astype(jnp.float32)
    q_home = (upstream * share_home[:, None]).astype(jnp.bfloat16)
    q_away = (upstream * share_away[:, None]).astype(jnp.bfloat16)
    gate_full, up_full, down_full = (
        lax.all_gather(w_gate, "replica", axis=1, tiled=True),
        lax.all_gather(w_up, "replica", axis=1, tiled=True),
        lax.all_gather(w_down, "replica", axis=1, tiled=True),
    )
    gate_w = gate_full.reshape(gate_full.shape[1], gate_full.shape[2])
    up_w = up_full.reshape(up_full.shape[1], up_full.shape[2])
    down_w = down_full.reshape(down_full.shape[1], down_full.shape[2])
    target = partner[:, 0]
    onehot_rows = (target[:, None] == jnp.arange(expert_count, dtype=jnp.int32)[None, :]).astype(
        jnp.int32
    )
    rank_within = jnp.sum((jnp.cumsum(onehot_rows, axis=0) - onehot_rows) * onehot_rows, axis=1)
    destination = target * capacity + rank_within
    placing = (
        jnp.arange(expert_count * capacity, dtype=jnp.int32)[:, None] == destination[None, :]
    ).astype(jnp.bfloat16)
    send_x = (
        jnp.dot(placing, tokens, preferred_element_type=jnp.float32)
        .astype(jnp.bfloat16)
        .reshape(expert_count, capacity, width)
    )
    send_q = (
        jnp.dot(placing, q_away, preferred_element_type=jnp.float32)
        .astype(jnp.bfloat16)
        .reshape(expert_count, capacity, width)
    )
    hidden_home, grad_home = expert_backward(tokens, q_home, gate_w, up_w, down_w)
    x_there = lax.all_to_all(send_x, "expert", split_axis=0, concat_axis=0, tiled=True)
    q_there = lax.all_to_all(send_q, "expert", split_axis=0, concat_axis=0, tiled=True)
    item_count = x_there.shape[1]
    hidden_there, grad_there = expert_backward(
        x_there.reshape(-1, width), q_there.reshape(-1, width), gate_w, up_w, down_w
    )
    returned = lax.all_to_all(
        grad_there.astype(jnp.bfloat16).reshape(expert_count, item_count, width),
        "expert",
        split_axis=0,
        concat_axis=0,
        tiled=True,
    )
    returned, hidden_away, q_there = (
        returned,
        hidden_there.reshape(expert_count, item_count, -1),
        q_there,
    )
    contract = (((0,), (0,)), ((), ()))
    flat_returned = returned.reshape(expert_count * capacity, width)
    grad_away = lax.dot_general(
        placing, flat_returned, contract, preferred_element_type=jnp.float32
    )
    token_grad = (grad_home + grad_away).astype(jnp.bfloat16)
    flat_hidden = hidden_away.reshape(expert_count * capacity, -1)
    flat_q = q_there.reshape(expert_count * capacity, width)
    grad_down = lax.psum_scatter(
        (
            lax.dot_general(hidden_home, q_home, contract, preferred_element_type=jnp.float32)
            + lax.dot_general(flat_hidden, flat_q, contract, preferred_element_type=jnp.float32)
        ).astype(jnp.bfloat16),
        "replica",
        scatter_dimension=0,
        tiled=True,
    )
    return (token_grad, grad_down[None])


def solution(mesh):
    placed = (
        P(("expert", "replica"), None),
        P(("expert", "replica"), None),
        P(("expert", "replica"), None),
        P(("expert", "replica"), None),
        P(("expert", "replica")),
        P("expert", "replica", None),
        P("expert", "replica", None),
        P("expert", "replica", None),
    )
    return jax.shard_map(
        local,
        mesh=mesh,
        in_specs=placed,
        out_specs=(P(("expert", "replica"), None), P("expert", "replica", None)),
        check_vma=False,
    )
```

profile of v0, /device:TPU:10, one launch (start us, length us, event | category | flops | bytes accessed | tf_op | source)
XLA Modules:
  0.0 331.8 jit_solution(12413700207397267182)
XLA Ops:
  10.7 0.7 fusion.45
  11.6 0.8 select_reduce_fusion
  13.1 1.5 convolution_convert_fusion.1
  14.7 1.2 reshape.51
  15.9 9.4 %all-to-all-start = ((bf16[32,5,2560]{2,1,0:T(8,128)(2,1)}), bf16[32,5,2560]{2,1,0:T(8,128)(2,1)S(1)}, u32[]{:S(2)}, u32[]{:S(2)}) async-start(bf16[32,5,2560]{2,1,0:T(8,128)(2,1)} %reshape.51), calls=%async_computation | async-start | bytes 2621440 | tf_op jit(solution)/shard_map/all_to_all | solution.py:71
  25.7 1.3 reshape.53
  27.1 15.6 %all-to-all-done = bf16[32,5,2560]{2,1,0:T(8,128)(2,1)S(1)} async-done(((bf16[32,5,2560]{2,1,0:T(8,128)(2,1)}), bf16[32,5,2560]{2,1,0:T(8,128)(2,1)S(1)}, u32[]{:S(2)}, u32[]{:S(2)}) %all-to-all-start) | async-done | bytes 819232 | tf_op jit(solution)/shard_map/all_to_all | solution.py:71
  42.7 7.1 %all-to-all-start.1 = ((bf16[32,5,2560]{2,1,0:T(8,128)(2,1)}), bf16[32,5,2560]{2,1,0:T(8,128)(2,1)}, u32[]{:S(2)}, u32[]{:S(2)}) async-start(bf16[32,5,2560]{2,1,0:T(8,128)(2,1)} %reshape.53), calls=%async_computation.1 | async-start | bytes 2621440 | tf_op jit(solution)/shard_map/all_to_all | solution.py:70
  50.2 16.9 %all-to-all-done.1 = bf16[32,5,2560]{2,1,0:T(8,128)(2,1)} async-done(((bf16[32,5,2560]{2,1,0:T(8,128)(2,1)}), bf16[32,5,2560]{2,1,0:T(8,128)(2,1)}, u32[]{:S(2)}, u32[]{:S(2)}) %all-to-all-start.1) | async-done | bytes 819232 | tf_op jit(solution)/shard_map/all_to_all | solution.py:70
  67.1 1.5 reshape.54
  68.6 23.4 %all-gather.8.cloned.1.call-done = bf16[1,2560,768]{2,1,0:T(8,128)(2,1)} async-done(((bf16[1,160,768]{2,1,0:T(8,128)(2,1)}), bf16[1,2560,768]{2,1,0:T(8,128)(2,1)}) %all-gather.8.cloned.1.call-update) | async-done | bytes 3932176 | tf_op jit(solution)/shard_map/all_gather | solution.py:43
  92.0 2.8 fusion.6
  94.8 73.8 %all-gather.6.cloned.1.call-done = bf16[1,2560,768]{2,1,0:T(8,128)(2,1)} async-done(((bf16[1,160,768]{2,1,0:T(8,128)(2,1)}), bf16[1,2560,768]{2,1,0:T(8,128)(2,1)}) %all-gather.6.cloned.1.call-update) | async-done | bytes 3932176 | tf_op jit(solution)/shard_map/all_gather | solution.py:44
  168.6 2.9 fusion.14
  171.6 3.1 fusion.2
  174.6 0.8 fusion.10
  175.7 1.3 fusion.36
  177.0 3.2 add_convert_fusion
  180.2 64.9 %all-gather.4.cloned.1.call-done = bf16[1,768,2560]{2,1,0:T(8,128)(2,1)} async-done(((bf16[1,48,2560]{2,1,0:T(8,128)(2,1)}), bf16[1,768,2560]{2,1,0:T(8,128)(2,1)}) %all-gather.4.cloned.1.call-update) | async-done | bytes 3932176 | tf_op jit(solution)/shard_map/all_gather | solution.py:45
  245.1 3.7 %fusion.16 = f32[160,768]{1,0:T(8,128)S(1)} fusion(bf16[160,2560]{1,0:T(8,128)(2,1)S(1)} %reshape.52, bf16[1,768,2560]{2,1,0:T(8,128)(2,1)} %all-gather.4.cloned.1.call-done), kind=kOutput, calls=%fused_computation.17 | convolution fusion | flops 629145600 | bytes 5242880 | tf_op jit(solution)/shard_map/dot_general | solution.py:8
  248.9 1.4 fusion
  251.0 1.4 fusion.26
  252.4 1.3 reshape.55
  253.7 7.6 %all-to-all-start.2 = ((bf16[32,5,2560]{2,1,0:T(8,128)(2,1)}), bf16[32,5,2560]{2,1,0:T(8,128)(2,1)}, u32[]{:S(2)}, u32[]{:S(2)}) async-start(bf16[32,5,2560]{2,1,0:T(8,128)(2,1)} %reshape.55), calls=%async_computation.2 | async-start | bytes 2621440 | tf_op jit(solution)/shard_map/all_to_all | solution.py:76
  261.3 3.7 %fusion.18 = f32[128,768]{1,0:T(8,128)S(1)} fusion(bf16[1,768,2560]{2,1,0:T(8,128)(2,1)} %all-gather.4.cloned.1.call-done, bf16[128,2560]{1,0:T(8,128)(2,1)S(1)} %copy-done.7, f32[128]{0:T(128)S(1)} %get-tuple-element.3), kind=kOutput, calls=%fused_computation.19 | convolution fusion | flops 504299520 | bytes 4981248 | tf_op jit(solution)/shard_map/dot_general | solution.py:8
  265.0 1.4 fusion.4
  266.4 0.7 copy-done.3
  267.1 1.4 fusion.23
  268.5 10.0 %all-to-all-done.2 = bf16[32,5,2560]{2,1,0:T(8,128)(2,1)} async-done(((bf16[32,5,2560]{2,1,0:T(8,128)(2,1)}), bf16[32,5,2560]{2,1,0:T(8,128)(2,1)}, u32[]{:S(2)}, u32[]{:S(2)}) %all-to-all-start.2) | async-done | bytes 819232 | tf_op jit(solution)/shard_map/all_to_all | solution.py:76
  278.5 1.5 reshape.56
  280.0 1.2 fusion.29
  281.2 44.0 %reduce-scatter.2.cloned.1.call-done = bf16[48,2560]{1,0:T(8,128)(2,1)} async-done(((bf16[768,2560]{1,0:T(8,128)(2,1)}), bf16[48,2560]{1,0:T(8,128)(2,1)}) %reduce-scatter.2.cloned.1.call-update) | async-done | bytes 245776 | tf_op jit(solution)/shard_map/reduce_scatter | solution.py:96
  (37 shorter events, 5.5 us)
Async XLA Ops:
  7.2 18.2 %copy-start = (bf16[128,2560]{1,0:T(8,128)(2,1)S(1)}, bf16[128,2560]{1,0:T(8,128)(2,1)}, u32[]{:S(2)}) copy-start(bf16[128,2560]{1,0:T(8,128)(2,1)} %param.8) | copy-start | bytes 1966084
  7.2 84.8 %all-gather.8.cloned.1.call-start = ((), (), s32[]{:S(2)}) async-start(), calls=%async_computation.6 | async-start | bytes 4177920 | tf_op jit(solution)/shard_map/all_gather | solution.py:43
  7.9 160.7 %all-gather.6.cloned.1.call-start = ((), (), s32[]{:S(2)}) async-start(), calls=%async_computation.5 | async-start | bytes 4177920 | tf_op jit(solution)/shard_map/all_gather | solution.py:44
  8.7 236.5 %all-gather.4.cloned.1.call-start = ((), (), s32[]{:S(2)}) async-start(), calls=%async_computation.4 | async-start | bytes 4177920 | tf_op jit(solution)/shard_map/all_gather | solution.py:45
  15.9 26.7 %all-to-all-start = ((bf16[32,5,2560]{2,1,0:T(8,128)(2,1)}), bf16[32,5,2560]{2,1,0:T(8,128)(2,1)S(1)}, u32[]{:S(2)}, u32[]{:S(2)}) async-start(bf16[32,5,2560]{2,1,0:T(8,128)(2,1)} %reshape.51), calls=%async_computation | async-start | bytes 2621440 | tf_op jit(solution)/shard_map/all_to_all | solution.py:71
  42.7 24.4 %all-to-all-start.1 = ((bf16[32,5,2560]{2,1,0:T(8,128)(2,1)}), bf16[32,5,2560]{2,1,0:T(8,128)(2,1)}, u32[]{:S(2)}, u32[]{:S(2)}) async-start(bf16[32,5,2560]{2,1,0:T(8,128)(2,1)} %reshape.53), calls=%async_computation.1 | async-start | bytes 2621440 | tf_op jit(solution)/shard_map/all_to_all | solution.py:70
  49.8 275.5 %reduce-scatter.2.cloned.1.call-start = ((), (), s32[]{:S(2)}) async-start(), calls=%async_computation.7 | async-start | bytes 4177920 | tf_op jit(solution)/shard_map/reduce_scatter | solution.py:96
  168.6 6.0 %copy-start.1 = (bf16[1,2560,768]{2,1,0:T(8,128)(2,1)S(1)}, bf16[1,2560,768]{2,1,0:T(8,128)(2,1)}, u32[]{:S(2)}) copy-start(bf16[1,2560,768]{2,1,0:T(8,128)(2,1)} %all-gather.6.cloned.1.call-done) | copy-start | bytes 11796484
  171.5 3.9 %copy-start.10 = (f32[128,768]{1,0:T(8,128)}, f32[128,768]{1,0:T(8,128)S(1)}, u32[]{:S(2)}) copy-start(f32[128,768]{1,0:T(8,128)S(1)} %fusion.14) | copy-start | bytes 1179652
  174.6 1.1 copy-start.6
  175.4 1.6 copy-start.8
  180.2 68.6 %copy-start.9 = (f32[160,768]{1,0:T(8,128)S(1)}, f32[160,768]{1,0:T(8,128)}, u32[]{:S(2)}) copy-start(f32[160,768]{1,0:T(8,128)} %copy-done.8) | copy-start | bytes 1474564
  245.1 3.7 %copy-start.4 = (bf16[1,2560,768]{2,1,0:T(8,128)(2,1)S(1)}, bf16[1,2560,768]{2,1,0:T(8,128)(2,1)}, u32[]{:S(2)}) copy-start(bf16[1,2560,768]{2,1,0:T(8,128)(2,1)} %all-gather.8.cloned.1.call-done) | copy-start | bytes 11796484
  248.9 2.1 copy-start.2
  252.4 8.9 %copy-start.7 = (bf16[128,2560]{1,0:T(8,128)(2,1)S(1)}, bf16[128,2560]{1,0:T(8,128)(2,1)}, u32[]{:S(2)}) copy-start(bf16[128,2560]{1,0:T(8,128)(2,1)} %param.9) | copy-start | bytes 1966084
  253.7 11.3 %copy-start.11 = (f32[128,768]{1,0:T(8,128)S(1)}, f32[128,768]{1,0:T(8,128)}, u32[]{:S(2)}) copy-start(f32[128,768]{1,0:T(8,128)} %copy-done.10) | copy-start | bytes 1179652
  253.7 24.9 %all-to-all-start.2 = ((bf16[32,5,2560]{2,1,0:T(8,128)(2,1)}), bf16[32,5,2560]{2,1,0:T(8,128)(2,1)}, u32[]{:S(2)}, u32[]{:S(2)}) async-start(bf16[32,5,2560]{2,1,0:T(8,128)(2,1)} %reshape.55), calls=%async_computation.2 | async-start | bytes 2621440 | tf_op jit(solution)/shard_map/all_to_all | solution.py:76
  261.3 3.7 %copy-start.5 = (bf16[1,2560,768]{2,1,0:T(8,128)(2,1)S(1)}, bf16[1,2560,768]{2,1,0:T(8,128)(2,1)}, u32[]{:S(2)}) copy-start(bf16[1,2560,768]{2,1,0:T(8,128)(2,1)} %all-gather.8.cloned.1.call-done) | copy-start | bytes 11796484
  265.0 2.1 copy-start.3
Sparse Core Ops, SparseCore 0:
  10.1 81.8 all-gather.7
  94.1 74.4 all-gather.5
  170.7 74.4 all-gather.3
  248.4 76.7 reduce-scatter.1
where the time goes:
time: 333 us; the launch traced here: 332 us
  waiting for transfers between devices  251 us (75%)
  matrix products  30.2 us (9%)
  starting transfers between devices  24.2 us (7%)
  between operations  14.7 us (4%)
  local copies, waits for them, and re-layouts  8.84 us (3%)
    all_gather x1, waiting for transfers between devices, local(): lax.all_gather(w_up, 'replica', axis=1, tiled=True)  73.8 us
    all_gather x1, waiting for transfers between devices, local(): lax.all_gather(w_down, 'replica', axis=1, tiled=True)  64.9 us
    reduce_scatter x1, waiting for transfers between devices, local(): lax.psum_scatter((lax.dot_general(hidden_home, q_home, contract, preferre...  44 us
    all_gather x1, waiting for transfers between devices, local(): lax.all_gather(w_gate, 'replica', axis=1, tiled=True)  23.4 us
    all_to_all x1, waiting for transfers between devices, local(): lax.all_to_all(send_x, 'expert', split_axis=0, concat_axis=0, tiled=True)  16.9 us
    all_to_all x1, waiting for transfers between devices, local(): lax.all_to_all(send_q, 'expert', split_axis=0, concat_axis=0, tiled=True)  15.6 us
    dot_general x6, matrix products, against_rows(): lax.dot_general(left, matrix, (((1,), (1,)), ((), ())), preferred_element...  13 us
    all_to_all x1, waiting for transfers between devices, local(): lax.all_to_all(grad_there.astype(jnp.bfloat16).reshape(expert_count, item...  9.99 us
  transfers between devices with their start and end apart: 7, of which 7 were waited for; matrix products, arithmetic and copies ran while one was open for 12% of the time, Pallas kernels for 0%

commit v1 on v0

--- a/solution.py
+++ b/solution.py
@@ -2,6 +2,12 @@
 import jax.numpy as jnp
 from jax import lax
 from jax.sharding import PartitionSpec as P
+
+
+def resolve_ticks_by_axis(my_data, axis_tag):
+    all_rows = jnp.stack([my_data for _ in range(lax.axis_size(axis_tag))], axis=0)
+    prior = jnp.concatenate(lax.all_to_all(all_rows, axis_tag, 0, 0), axis=1)
+    return prior
 
 
 def against_rows(left, matrix):
@@ -41,7 +47,7 @@
     q_away = (upstream * share_away[:, None]).astype(jnp.bfloat16)
     gate_full, up_full, down_full = (
         lax.all_gather(w_gate, "replica", axis=1, tiled=True),
-        lax.all_gather(w_up, "replica", axis=1, tiled=True),
+        resolve_ticks_by_axis(w_up, "replica"),
         lax.all_gather(w_down, "replica", axis=1, tiled=True),
     )
     gate_w = gate_full.reshape(gate_full.shape[1], gate_full.shape[2])

time: 333 us -> 461 us (1.38)
  the two profiles are of different devices: /device:TPU:10 before, /device:TPU:2 now
where the time goes in v1:
time: 461 us; the launch traced here: 460 us
  waiting for transfers between devices  340 us (74%)
  matrix products  35.8 us (8%)
  starting transfers between devices  30.6 us (7%)
  blocking collectives  26.1 us (6%)
  between operations  14.7 us (3%)
  local copies, waits for them, and re-layouts  9.78 us (2%)
    all_gather x1, waiting for transfers between devices, local(): lax.all_gather(w_gate, 'replica', axis=1, tiled=True)  213 us
    all_gather x1, waiting for transfers between devices, local(): lax.all_gather(w_down, 'replica', axis=1, tiled=True)  59.4 us
    reduce_scatter x1, waiting for transfers between devices, local(): lax.psum_scatter((lax.dot_general(hidden_home, q_home, contract, preferre...  39.4 us
    all_to_all x1, blocking collectives, local(): lax.all_to_all(send_x, 'expert', split_axis=0, concat_axis=0, tiled=True)  26.1 us
    dot_general x6, matrix products, against_rows(): lax.dot_general(left, matrix, (((1,), (1,)), ((), ())), preferred_element...  17.2 us
    all_to_all x1, waiting for transfers between devices, local(): lax.all_to_all(send_q, 'expert', split_axis=0, concat_axis=0, tiled=True)  15.6 us
    all_to_all x1, starting transfers between devices, resolve_ticks_by_axis(): prior = jnp.concatenate(lax.all_to_all(all_rows, axis_tag, 0, 0), axis=1)  13.3 us
    all_to_all x1, waiting for transfers between devices, local(): lax.all_to_all(grad_there.astype(jnp.bfloat16).reshape(expert_count, item...  11 us
  transfers between devices with their start and end apart: 6, of which 5 were waited for; matrix products, arithmetic and copies ran while one was open for 9% of the time, Pallas kernels for 0%

profile of v1, /device:TPU:2, one launch (start us, length us, event | category | flops | bytes accessed | tf_op | source)
XLA Modules:
  0.0 460.0 jit_solution(14648983725689794678)
XLA Ops:
  7.9 0.7 convert_element_type.50
  8.6 0.7 fusion.39
  9.5 0.8 select_reduce_fusion
  11.0 1.5 convolution_convert_fusion.1
  12.5 1.2 reshape.50
  13.8 9.7 %all-to-all-start.1 = ((bf16[32,5,2560]{2,1,0:T(8,128)(2,1)}), bf16[32,5,2560]{2,1,0:T(8,128)(2,1)S(1)}, u32[]{:S(2)}, u32[]{:S(2)}) async-start(bf16[32,5,2560]{2,1,0:T(8,128)(2,1)} %reshape.50), calls=%async_computation.1 | async-start | bytes 2621440 | tf_op jit(solution)/shard_map/all_to_all | solution.py:77
  23.8 1.3 reshape.52
  25.1 15.6 %all-to-all-done.1 = bf16[32,5,2560]{2,1,0:T(8,128)(2,1)S(1)} async-done(((bf16[32,5,2560]{2,1,0:T(8,128)(2,1)}), bf16[32,5,2560]{2,1,0:T(8,128)(2,1)S(1)}, u32[]{:S(2)}, u32[]{:S(2)}) %all-to-all-start.1) | async-done | bytes 819232 | tf_op jit(solution)/shard_map/all_to_all | solution.py:77
  40.7 26.1 %all_to_all.20 = bf16[32,5,2560]{2,1,0:T(8,128)(2,1)} all-to-all(bf16[32,5,2560]{2,1,0:T(8,128)(2,1)} %reshape.52), channel_id=1, replica_groups=mesh['expert'=32,'replica'=16] {'expert'}, dimensions={0} | all-to-all | bytes 1638400 | tf_op jit(solution)/shard_map/all_to_all | solution.py:76
  66.9 2.3 stack.2
  69.2 13.3 %all-to-all-start = ((bf16[16,1,160,768]{3,2,1,0:T(8,128)(2,1)}), bf16[16,1,160,768]{3,2,1,0:T(8,128)(2,1)}, u32[]{:S(2)}, u32[]{:S(2)}) async-start(bf16[16,1,160,768]{3,2,1,0:T(8,128)(2,1)} %stack.2), calls=%async_computation | async-start | bytes 7864320 | tf_op jit(solution)/shard_map/all_to_all | solution.py:9
  83.3 0.7 all-gather.3.cloned.1.call-update
  84.4 1.5 reshape.53
  85.9 213.0 %all-gather.5.cloned.1.call-done = bf16[1,2560,768]{2,1,0:T(8,128)(2,1)} async-done(((bf16[1,160,768]{2,1,0:T(8,128)(2,1)}), bf16[1,2560,768]{2,1,0:T(8,128)(2,1)}) %all-gather.5.cloned.1.call-update) | async-done | bytes 3932176 | tf_op jit(solution)/shard_map/all_gather | solution.py:49
  298.9 2.9 fusion.6
  302.2 0.8 fusion.2
  303.0 2.9 fusion.51
  305.9 3.1 fusion.52
  309.0 1.3 fusion.28
  310.3 3.2 add_convert_fusion
  313.5 59.4 %all-gather.3.cloned.1.call-done = bf16[1,768,2560]{2,1,0:T(8,128)(2,1)} async-done(((bf16[1,48,2560]{2,1,0:T(8,128)(2,1)}), bf16[1,768,2560]{2,1,0:T(8,128)(2,1)}) %all-gather.3.cloned.1.call-update) | async-done | bytes 3932176 | tf_op jit(solution)/shard_map/all_gather | solution.py:51
  372.9 3.7 fusion.10
  376.6 1.4 fusion.8
  378.0 3.7 fusion.31
  381.7 2.3 fusion.18
  384.0 2.3 reshape.54
  386.3 7.6 %all-to-all-start.3 = ((bf16[32,5,2560]{2,1,0:T(8,128)(2,1)}), bf16[32,5,2560]{2,1,0:T(8,128)(2,1)S(1)}, u32[]{:S(2)}, u32[]{:S(2)}) async-start(bf16[32,5,2560]{2,1,0:T(8,128)(2,1)} %reshape.54), calls=%async_computation.3 | async-start | bytes 2621440 | tf_op jit(solution)/shard_map/all_to_all | solution.py:82
  393.9 3.6 fusion.33
  397.6 2.5 fusion.15
  400.1 11.0 %all-to-all-done.3 = bf16[32,5,2560]{2,1,0:T(8,128)(2,1)S(1)} async-done(((bf16[32,5,2560]{2,1,0:T(8,128)(2,1)}), bf16[32,5,2560]{2,1,0:T(8,128)(2,1)S(1)}, u32[]{:S(2)}, u32[]{:S(2)}) %all-to-all-start.3) | async-done | bytes 819232 | tf_op jit(solution)/shard_map/all_to_all | solution.py:82
  411.5 2.5 fusion.21
  414.0 39.4 %reduce-scatter.2.cloned.1.call-done = bf16[48,2560]{1,0:T(8,128)(2,1)} async-done(((bf16[768,2560]{1,0:T(8,128)(2,1)}), bf16[48,2560]{1,0:T(8,128)(2,1)}) %reduce-scatter.2.cloned.1.call-update) | async-done | bytes 245776 | tf_op jit(solution)/shard_map/reduce_scatter | solution.py:102
  (36 shorter events, 3.2 us)
Async XLA Ops:
  7.2 16.3 %copy-start = (bf16[128,2560]{1,0:T(8,128)(2,1)S(1)}, bf16[128,2560]{1,0:T(8,128)(2,1)}, u32[]{:S(2)}) copy-start(bf16[128,2560]{1,0:T(8,128)(2,1)} %param.8) | copy-start | bytes 1966084
  13.8 53.1 %copy-start.11 = (bf16[1,160,768]{2,1,0:T(8,128)(2,1)S(1)}, bf16[1,160,768]{2,1,0:T(8,128)(2,1)}, u32[]{:S(2)}) copy-start(bf16[1,160,768]{2,1,0:T(8,128)(2,1)} %param.14) | copy-start | bytes 737284
  13.8 27.0 %all-to-all-start.1 = ((bf16[32,5,2560]{2,1,0:T(8,128)(2,1)}), bf16[32,5,2560]{2,1,0:T(8,128)(2,1)S(1)}, u32[]{:S(2)}, u32[]{:S(2)}) async-start(bf16[32,5,2560]{2,1,0:T(8,128)(2,1)} %reshape.50), calls=%async_computation.1 | async-start | bytes 2621440 | tf_op jit(solution)/shard_map/all_to_all | solution.py:77
  69.2 233.8 %all-to-all-start = ((bf16[16,1,160,768]{3,2,1,0:T(8,128)(2,1)}), bf16[16,1,160,768]{3,2,1,0:T(8,128)(2,1)}, u32[]{:S(2)}, u32[]{:S(2)}) async-start(bf16[16,1,160,768]{3,2,1,0:T(8,128)(2,1)} %stack.2), calls=%async_computation | async-start | bytes 7864320 | tf_op jit(solution)/shard_map/all_to_all | solution.py:9
  82.5 216.4 %all-gather.5.cloned.1.call-start = ((), (), s32[]{:S(2)}) async-start(), calls=%async_computation.6 | async-start | bytes 4177920 | tf_op jit(solution)/shard_map/all_gather | solution.py:49
  83.2 289.6 %all-gather.3.cloned.1.call-start = ((), (), s32[]{:S(2)}) async-start(), calls=%async_computation.5 | async-start | bytes 4177920 | tf_op jit(solution)/shard_map/all_gather | solution.py:51
  84.0 369.4 %reduce-scatter.2.cloned.1.call-start = ((), (), s32[]{:S(2)}) async-start(), calls=%async_computation.7 | async-start | bytes 4177920 | tf_op jit(solution)/shard_map/reduce_scatter | solution.py:102
  298.9 3.3 copy-start.1
  303.0 6.0 %copy-start.5 = (bf16[128,2560]{1,0:T(8,128)(2,1)S(1)}, bf16[128,2560]{1,0:T(8,128)(2,1)}, u32[]{:S(2)}) copy-start(bf16[128,2560]{1,0:T(8,128)(2,1)} %param.9) | copy-start | bytes 1966084
  305.9 3.1 copy-start.9
  308.9 1.3 copy-start.7
  313.5 59.4 %copy-start.6 = (bf16[128,2560]{1,0:T(8,128)(2,1)S(1)}, bf16[128,2560]{1,0:T(8,128)(2,1)}, u32[]{:S(2)}) copy-start(bf16[128,2560]{1,0:T(8,128)(2,1)} %param.9) | copy-start | bytes 1966084
  372.9 3.7 copy-start.4
  378.0 3.7 copy-start.2
  378.0 3.7 copy-start.8
  386.3 11.3 %copy-start.10 = (f32[128,768]{1,0:T(8,128)S(1)}, f32[128,768]{1,0:T(8,128)}, u32[]{:S(2)}) copy-start(f32[128,768]{1,0:T(8,128)} %copy-done.9) | copy-start | bytes 1179652
  386.3 24.8 %all-to-all-start.3 = ((bf16[32,5,2560]{2,1,0:T(8,128)(2,1)}), bf16[32,5,2560]{2,1,0:T(8,128)(2,1)S(1)}, u32[]{:S(2)}, u32[]{:S(2)}) async-start(bf16[32,5,2560]{2,1,0:T(8,128)(2,1)} %reshape.54), calls=%async_computation.3 | async-start | bytes 2621440 | tf_op jit(solution)/shard_map/all_to_all | solution.py:82
  393.9 3.7 copy-start.3
Sparse Core Ops, SparseCore 0:
  85.4 213.4 all-gather.4
  301.0 71.8 all-gather.2
  376.3 77.0 reduce-scatter.1
